TPU v7x, 32 devices: a whole 2x2x4 slice. The times are simulated.
32 devices in a mesh: chan: 4 (over y, x), tm: 8 (over z, core).
Axes of the slice: x: 2, y: 2, z: 4, core: 2. Of those that a mesh axis runs over, the one named last changes fastest.
Arguments:
- raw_samples: float32 [32, 512, 2048], P('tm', 'chan'), may hold values from -80 to 80
Outputs:
- correlations: float32 [512, 512, 256], P(('chan', 'tm'))
All inputs are finite; a program needn't handle non-finite values.
Results may differ from a plain program's by a relative error of at most 0.0043.
Values may be sent and summed in bfloat16 or wider, within the bound.
No kernel may reach another device: no remote copies, remote signals or barrier semaphores. Data moves between devices by JAX's collectives and lax.ppermute only.
A program may use at most 192 MiB of HBM per device.

v0:
```python
import math
import jax
import jax.numpy as jnp
from jax import lax
from jax.sharding import PartitionSpec as P

LAGS = 256


def spread(value, axis, source):
    kept = jnp.where(lax.axis_index(axis) == source, value, 0).astype(value.dtype)
    return lax.psum(kept, axis)


def decimate(raw_samples):
    even_taps = raw_samples[..., 0::2]
    odd_taps = raw_samples[..., 1::2]
    odd_before = jnp.concatenate([jnp.zeros_like(odd_taps[..., :1]), odd_taps[..., :-1]], axis=-1)
    return 0.25 * odd_before + 0.5 * even_taps + 0.25 * odd_taps


def whiten(real_part, imag_part):
    power = real_part * real_part + imag_part * imag_part
    level = jnp.mean(power, axis=-1, keepdims=True)
    factor = 1.0 / jnp.sqrt(power + 0.1 * level + 1e-06)
    return (real_part * factor, imag_part * factor)


def lag_table(freq_count, sample_count, lag_count):
    freq_index = jnp.arange(1, freq_count + 1, dtype=jnp.int32)
    lag_index = jnp.arange(lag_count, dtype=jnp.int32) - lag_count // 2
    turns = freq_index[:, None] * (lag_index[None, :] % sample_count) % sample_count
    angle = turns.astype(jnp.float32) * (2.0 * math.pi / sample_count)
    return jnp.concatenate([jnp.cos(angle), -jnp.sin(angle)], axis=0).astype(jnp.bfloat16)


def transform_tables(sample_count, freq_count):
    time_index = jnp.arange(sample_count, dtype=jnp.int32)
    freq_index = jnp.arange(1, freq_count + 1, dtype=jnp.int32)
    turns = time_index[:, None] * freq_index[None, :] % sample_count
    angle = turns.astype(jnp.float32) * (2.0 * math.pi / sample_count)
    return (jnp.cos(angle), -jnp.sin(angle))


def cross_block(local_spec, turned_spec, remote_spec):
    real_cross = jnp.einsum(
        "sik,sjk->ijk", local_spec, remote_spec, preferred_element_type=jnp.float32
    )
    imag_cross = jnp.einsum(
        "sik,sjk->ijk", turned_spec, remote_spec, preferred_element_type=jnp.float32
    )
    return jnp.concatenate([real_cross, imag_cross], axis=-1).astype(jnp.bfloat16)


def per_device(raw_samples):
    seg_count, block_width, raw_length = raw_samples.shape
    sample_count = raw_length // 2
    freq_count = sample_count // 8
    chan_count = lax.axis_size("chan")
    time_count = lax.axis_size("tm")
    channel_total = block_width * chan_count
    signal = decimate(raw_samples).reshape(seg_count * block_width, sample_count)
    cos_table, sin_table = transform_tables(sample_count, freq_count)
    real_part = jnp.dot(
        signal, cos_table, precision=lax.Precision.HIGHEST, preferred_element_type=jnp.float32
    )
    imag_part = jnp.dot(
        signal, sin_table, precision=lax.Precision.HIGHEST, preferred_element_type=jnp.float32
    )
    real_part = real_part.reshape(seg_count, block_width, freq_count)
    imag_part = imag_part.reshape(seg_count, block_width, freq_count)
    real_w, imag_w = whiten(real_part, imag_part)
    local_spec = jnp.concatenate([real_w, imag_w], axis=0).astype(jnp.bfloat16)
    table = lag_table(freq_count, sample_count, LAGS)
    norm_scale = 1.0 / math.sqrt(freq_count * seg_count * time_count)
    tm_index = lax.axis_index("tm")
    pair_spec = local_spec.reshape(2, seg_count, block_width, freq_count)
    all_spec = lax.all_gather(pair_spec, "tm", axis=1, tiled=True)
    span_width = channel_total // time_count
    span_offset = tm_index * span_width % block_width
    own_span = lax.dynamic_slice_in_dim(all_spec, span_offset, span_width, 2)
    root_block = tm_index * span_width // block_width
    column_spec = spread(own_span, "chan", root_block)

    def add_group(group_index, total):
        seg_start = (group_index * seg_count).astype(jnp.int32)
        left_group = lax.dynamic_slice_in_dim(all_spec, seg_start, seg_count, 1)
        right_group = lax.dynamic_slice_in_dim(column_spec, seg_start, seg_count, 1)
        left_rows = left_group.reshape(2 * seg_count, block_width, freq_count)
        turned_rows = jnp.concatenate([left_group[1], -left_group[0]], axis=0)
        right_rows = right_group.reshape(2 * seg_count, span_width, freq_count)
        return total + cross_block(left_rows, turned_rows, right_rows).astype(jnp.float32)

    summed = lax.fori_loop(
        0, time_count, add_group, jnp.zeros((block_width, span_width, 2 * freq_count), jnp.float32)
    )
    pair_lags = (
        jnp.einsum(
            "ijk,kl->ijl", summed, table.astype(jnp.float32), precision=lax.Precision.HIGHEST
        )
        * norm_scale
    )
    return lax.all_to_all(pair_lags, "tm", split_axis=0, concat_axis=1, tiled=True)


def solution(mesh):
    return jax.shard_map(
        per_device,
        mesh=mesh,
        in_specs=(P("tm", "chan", None),),
        out_specs=P(("chan", "tm"), None, None),
        check_vma=False,
    )
```

profile of v0, /device:TPU:0, one launch (start us, length us, event | category | flops | bytes accessed | tf_op | source)
XLA Modules:
  0.0 571.0 jit_solution(17318905619053049182)
XLA Ops:
  6.5 70.9 %slice.23 = f32[4,128,1024]{2,1,0:T(8,128)S(1)} slice(f32[4,128,2048]{2,1,0:T(8,128)} %param.3), slice={[0:4:1], [0:128:1], [1:2048:2]} | slice | bytes 4194304 | tf_op jit(solution)/shard_map/slice | solution.py:17
  77.4 71.3 %slice.25 = f32[4,128,1024]{2,1,0:T(8,128)} slice(f32[4,128,2048]{2,1,0:T(8,128)} %param.3), slice={[0:4:1], [0:128:1], [0:2048:2]} | slice | bytes 4194304 | tf_op jit(solution)/shard_map/slice | solution.py:16
  148.7 6.3 %fusion.13 = f32[4,128,128]{1,2,0:T(8,128)S(1)} fusion(s32[128]{0:T(128)S(1)} %iota_add_fusion, f32[4,128,1024]{2,1,0:T(8,128)S(1)} %slice.23, f32[4,128,1024]{2,1,0:T(8,128)} %slice.25, f32[4,128,1023]{2,1,0:T(8,128)S(1)} %bitcast.48), kind=kOutput, calls=%fused_computation.24 | convolution fusion | flops 809762816 | bytes 6552064 | tf_op jit(solution)/shard_map/dot_general | solution.py:64
  155.1 4.7 fusion.23
  160.9 31.9 %all-gather.2.cloned.1.call-done = bf16[2,32,128,128]{3,2,0,1:T(8,128)(2,1)} async-done(((bf16[2,4,128,128]{3,2,0,1:T(8,128)(2,1)}), bf16[2,32,128,128]{3,2,0,1:T(8,128)(2,1)}) %all-gather.2.cloned.1.call-update) | async-done | bytes 2097168 | tf_op jit(solution)/shard_map/all_gather | solution.py:78
  192.7 2.6 dynamic-slice_select_fusion
  196.0 51.9 %all-reduce.3.cloned.1.call-done = bf16[2,32,64,128]{3,2,0,1:T(8,128)(2,1)} async-done(((bf16[2,32,64,128]{3,2,0,1:T(8,128)(2,1)}), bf16[2,32,64,128]{3,2,0,1:T(8,128)(2,1)}) %all-reduce.3.cloned.1.call-update) | async-done | bytes 1048592 | tf_op jit(solution)/shard_map/psum | solution.py:12
  247.9 104.6 %while.14 = (s32[]{:T(128)}, f32[128,64,256]{0,1,2:T(8,128)}, bf16[2,32,64,128]{3,2,0,1:T(8,128)(2,1)}, bf16[2,32,128,128]{3,2,0,1:T(8,128)(2,1)}, s32[]{:T(128)}, /*index=5*/s32[]{:T(128)}, s32[]{:T(128)}, s32[]{:T(128)}, s32[]{}) while((s32[]{:T(128)}, f32[128,64,256]{0,1,2:T(8,128)}, bf16[2,32,64,128]{3,2,0,1:T(8,128)(2,1)}, ...), condition=%wide.region_3.4_spmd.clone, body=%wide.region_2.3_spmd.clone.sunk | while | flops 44630024 | bytes 28573872 | solution.py:94
  247.9 1.0 constant_dynamic-slice_fusion.7
  252.2 2.1 convert_bitcast_fusion.5
  254.3 5.3 select_add_fusion.2
  259.6 1.0 constant_dynamic-slice_fusion.7
  264.0 2.1 convert_bitcast_fusion.5
  266.0 6.8 %select_add_fusion.2 = f32[128,64,256]{0,1,2:T(8,128)} fusion(f32[128,64,256]{0,1,2:T(8,128)} %get-tuple-element.163, bf16[128,64,128]{0,1,2:T(8,128)(2,1)S(1)} %convert_bitcast_fusion.4, bf16[128,64,128]{0,1,2:T(8,128)(2,1)} %convert_bitcast_fusion.5, pred[]{:T(512)S(6)} %compare.13), kind=kLoop, calls=%fused_computation.clone.1 | loop fusion | flops 8388608 | bytes 20971520 | tf_op jit(solution)/shard_map/while/body/eval_jaxpr/add | solution.py:92
  272.9 1.0 constant_dynamic-slice_fusion.7
  277.2 2.1 convert_bitcast_fusion.5
  279.3 6.8 %select_add_fusion.2 = f32[128,64,256]{0,1,2:T(8,128)} fusion(f32[128,64,256]{0,1,2:T(8,128)} %get-tuple-element.163, bf16[128,64,128]{0,1,2:T(8,128)(2,1)S(1)} %convert_bitcast_fusion.4, bf16[128,64,128]{0,1,2:T(8,128)(2,1)} %convert_bitcast_fusion.5, pred[]{:T(512)S(6)} %compare.13), kind=kLoop, calls=%fused_computation.clone.1 | loop fusion | flops 8388608 | bytes 20971520 | tf_op jit(solution)/shard_map/while/body/eval_jaxpr/add | solution.py:92
  286.1 1.0 constant_dynamic-slice_fusion.7
  290.5 2.1 convert_bitcast_fusion.5
  292.6 6.8 %select_add_fusion.2 = f32[128,64,256]{0,1,2:T(8,128)} fusion(f32[128,64,256]{0,1,2:T(8,128)} %get-tuple-element.163, bf16[128,64,128]{0,1,2:T(8,128)(2,1)S(1)} %convert_bitcast_fusion.4, bf16[128,64,128]{0,1,2:T(8,128)(2,1)} %convert_bitcast_fusion.5, pred[]{:T(512)S(6)} %compare.13), kind=kLoop, calls=%fused_computation.clone.1 | loop fusion | flops 8388608 | bytes 20971520 | tf_op jit(solution)/shard_map/while/body/eval_jaxpr/add | solution.py:92
  303.8 2.1 convert_bitcast_fusion.5
  305.8 6.8 %select_add_fusion.2 = f32[128,64,256]{0,1,2:T(8,128)} fusion(f32[128,64,256]{0,1,2:T(8,128)} %get-tuple-element.163, bf16[128,64,128]{0,1,2:T(8,128)(2,1)S(1)} %convert_bitcast_fusion.4, bf16[128,64,128]{0,1,2:T(8,128)(2,1)} %convert_bitcast_fusion.5, pred[]{:T(512)S(6)} %compare.13), kind=kLoop, calls=%fused_computation.clone.1 | loop fusion | flops 8388608 | bytes 20971520 | tf_op jit(solution)/shard_map/while/body/eval_jaxpr/add | solution.py:92
  317.0 2.1 convert_bitcast_fusion.5
  319.1 6.8 %select_add_fusion.2 = f32[128,64,256]{0,1,2:T(8,128)} fusion(f32[128,64,256]{0,1,2:T(8,128)} %get-tuple-element.163, bf16[128,64,128]{0,1,2:T(8,128)(2,1)S(1)} %convert_bitcast_fusion.4, bf16[128,64,128]{0,1,2:T(8,128)(2,1)} %convert_bitcast_fusion.5, pred[]{:T(512)S(6)} %compare.13), kind=kLoop, calls=%fused_computation.clone.1 | loop fusion | flops 8388608 | bytes 20971520 | tf_op jit(solution)/shard_map/while/body/eval_jaxpr/add | solution.py:92
  330.3 2.1 convert_bitcast_fusion.5
  332.4 6.8 %select_add_fusion.2 = f32[128,64,256]{0,1,2:T(8,128)} fusion(f32[128,64,256]{0,1,2:T(8,128)} %get-tuple-element.163, bf16[128,64,128]{0,1,2:T(8,128)(2,1)S(1)} %convert_bitcast_fusion.4, bf16[128,64,128]{0,1,2:T(8,128)(2,1)} %convert_bitcast_fusion.5, pred[]{:T(512)S(6)} %compare.13), kind=kLoop, calls=%fused_computation.clone.1 | loop fusion | flops 8388608 | bytes 20971520 | tf_op jit(solution)/shard_map/while/body/eval_jaxpr/add | solution.py:92
  343.6 2.1 convert_bitcast_fusion.5
  345.6 6.8 %select_add_fusion.2 = f32[128,64,256]{0,1,2:T(8,128)} fusion(f32[128,64,256]{0,1,2:T(8,128)} %get-tuple-element.163, bf16[128,64,128]{0,1,2:T(8,128)(2,1)S(1)} %convert_bitcast_fusion.4, bf16[128,64,128]{0,1,2:T(8,128)(2,1)} %convert_bitcast_fusion.5, pred[]{:T(512)S(6)} %compare.13), kind=kLoop, calls=%fused_computation.clone.1 | loop fusion | flops 8388608 | bytes 20971520 | tf_op jit(solution)/shard_map/while/body/eval_jaxpr/add | solution.py:92
  352.5 14.2 %broadcast_multiply_fusion = f32[128,64,256]{2,0,1:T(8,128)S(1)} fusion(f32[128,64,256]{0,1,2:T(8,128)} %get-tuple-element.84, bf16[128,256]{1,0:T(8,128)(2,1)S(1)} %get-tuple-element.121, bf16[128,256]{1,0:T(8,128)(2,1)S(1)} %get-tuple-element.120), kind=kOutput, calls=%fused_computation.13 | convolution fusion | flops 6444810240 | bytes 16908288 | tf_op jit(solution)/shard_map/ijk,kl->ijl/dot_general | solution.py:98
  366.7 4.9 copy.12
  371.6 188.5 %all_to_all.18 = f32[128,64,256]{2,1,0:T(8,128)S(1)} all-to-all(f32[128,64,256]{2,1,0:T(8,128)S(1)} %copy.12), channel_id=1, replica_groups=mesh['chan'=4,'tm'=8] {'tm'}, dimensions={0} | all-to-all | bytes 16777216 | tf_op jit(solution)/shard_map/all_to_all | solution.py:103
  560.1 4.0 copy.13
  (74 shorter events, 32.2 us)
Async XLA Ops:
  6.5 186.2 %all-gather.2.cloned.1.call-start = ((), (), s32[]{:S(2)}) async-start(), calls=%async_computation.1 | async-start | bytes 2359296 | tf_op jit(solution)/shard_map/all_gather | solution.py:78
  148.7 6.3 %copy-start = (f32[4,128,1024]{2,1,0:T(8,128)S(1)}, f32[4,128,1024]{2,1,0:T(8,128)}, u32[]{:S(2)}) copy-start(f32[4,128,1024]{2,1,0:T(8,128)} %slice.25) | copy-start | bytes 6291460
  160.8 87.1 %all-reduce.3.cloned.1.call-start = ((), (), s32[]{:S(2)}) async-start(), calls=%async_computation.2 | async-start | bytes 2097152 | tf_op jit(solution)/shard_map/psum | solution.py:12
Sparse Core Ops, SparseCore 0:
  160.9 31.7 all-gather.1
  195.8 52.0 all-reduce.2
where the time goes:
time: 572 us; the launch traced here: 571 us
  blocking collectives  189 us (33%)
  local copies, waits for them, and re-layouts  172 us (30%)
  waiting for transfers between devices  83.8 us (15%)
  other arithmetic  64.5 us (11%)
  matrix products  47.8 us (8%)
  between operations  13.5 us (2%)
    all_to_all x1, blocking collectives, per_device(): lax.all_to_all(pair_lags, 'tm', split_axis=0, concat_axis=1, tiled=True)  189 us
    slice x1, local copies, waits for them, and re-layouts, decimate(): even_taps = raw_samples[..., 0::2]  71.3 us
    slice x1, local copies, waits for them, and re-layouts, decimate(): odd_taps = raw_samples[..., 1::2]  70.9 us
    add x8, other arithmetic, add_group(): total + cross_block(left_rows, turned_rows, right_rows).astype(jnp.float32)  53.2 us
    psum x1, waiting for transfers between devices, spread(): return lax.psum(kept, axis)  51.9 us
    all_gather x1, waiting for transfers between devices, per_device(): all_spec = lax.all_gather(pair_spec, 'tm', axis=1, tiled=True)  31.9 us
    dot_general x8, matrix products, cross_block(): jnp.einsum('sik,sjk->ijk', local_spec, remote_spec, preferred_element_typ...  16.6 us
    dot_general x1, matrix products, per_device(): jnp.einsum('ijk,kl->ijl', summed, table.astype(jnp.float32), precision=la...  14.2 us
  transfers between devices with their start and end apart: 2, of which 2 were waited for; matrix products, arithmetic and copies ran while one was open for 0% of the time, Pallas kernels for 0%

commit v1 on v0

--- a/solution.py
+++ b/solution.py
@@ -75,7 +75,22 @@
     norm_scale = 1.0 / math.sqrt(freq_count * seg_count * time_count)
     tm_index = lax.axis_index("tm")
     pair_spec = local_spec.reshape(2, seg_count, block_width, freq_count)
-    all_spec = lax.all_gather(pair_spec, "tm", axis=1, tiled=True)
+    ways, here, step = (lax.axis_size("tm"), lax.axis_index("tm"), pair_spec.shape[1])
+    lengths = [n * ways if d == 1 else n for d, n in enumerate(pair_spec.shape)]
+    all_spec = lax.dynamic_update_slice_in_dim(
+        jnp.zeros(lengths, pair_spec.dtype), pair_spec, here * step, axis=1
+    )
+    going_up = going_down = pair_spec
+    for far in range(1, ways // 2 + 1):
+        going_up = lax.ppermute(going_up, "tm", [(d, (d + 1) % ways) for d in range(ways)])
+        all_spec = lax.dynamic_update_slice_in_dim(
+            all_spec, going_up, (here - far) % ways * step, axis=1
+        )
+        if 2 * far < ways:
+            going_down = lax.ppermute(going_down, "tm", [(d, (d - 1) % ways) for d in range(ways)])
+            all_spec = lax.dynamic_update_slice_in_dim(
+                all_spec, going_down, (here + far) % ways * step, axis=1
+            )
     span_width = channel_total // time_count
     span_offset = tm_index * span_width % block_width
     own_span = lax.dynamic_slice_in_dim(all_spec, span_offset, span_width, 2)

time: 572 us -> 592 us (1.035)
  starting transfers between devices: 0.04 us -> 12.1 us
  local copies, waits for them, and re-layouts: 172 us -> 180 us
    all_gather x1 -> x0, waiting for transfers between devices: 31.9 us -> none  [per_device(): all_spec = lax.all_gather(pair_spec, 'tm', axis=1, tiled=True)]
    psum x1, waiting for transfers between devices: 51.9 us -> 69.2 us  [spread(): return lax.psum(kept, axis)]
    ppermute x0 -> x7, waiting for transfers between devices: none -> 13.3 us  [the longest x4 10.2 us: per_device(): lax.ppermute(going_up, 'tm', [(d, (d + 1) % ways) for d in range(ways)])]
    ppermute x0 -> x7, starting transfers between devices: none -> 12.1 us  [the longest x3 11.6 us: per_device(): lax.ppermute(going_down, 'tm', [(d, (d - 1) % ways) for d in range(ways)])]
    squeeze x0 -> x8, other arithmetic: none -> 9.54 us  [add_group(): turned_rows = jnp.concatenate([left_group[1], -left_group[0]], axis=0)]
    slice x8 -> x0, other arithmetic: 7.96 us -> none  [add_group(): turned_rows = jnp.concatenate([left_group[1], -left_group[0]], axis=0)]
    dynamic_update_slice x0 -> x8, local copies, waits for them, and re-layouts: none -> 6.65 us  [the longest x4 3.35 us: per_device(): lax.dynamic_update_slice_in_dim(all_spec, going_up, (here - far) % ways *...]
  transfers between devices with their start and end apart: 2 -> 8, of which waited for: 2 -> 7; matrix products, arithmetic and copies ran while one was open for 0% -> 1% of each run, Pallas kernels for 0% -> 0%
where the time goes in v1:
time: 592 us; the launch traced here: 591 us
  blocking collectives  189 us (32%)
  local copies, waits for them, and re-layouts  180 us (30%)
  waiting for transfers between devices  82.5 us (14%)
  other arithmetic  67.3 us (11%)
  matrix products  46.8 us (8%)
  between operations  13.5 us (2%)
  starting transfers between devices  12.1 us (2%)
    all_to_all x1, blocking collectives, per_device(): lax.all_to_all(pair_lags, 'tm', split_axis=0, concat_axis=1, tiled=True)  189 us
    slice x1, local copies, waits for them, and re-layouts, decimate(): even_taps = raw_samples[..., 0::2]  71.3 us
    slice x1, local copies, waits for them, and re-layouts, decimate(): odd_taps = raw_samples[..., 1::2]  70.9 us
    psum x1, waiting for transfers between devices, spread(): return lax.psum(kept, axis)  69.2 us
    add x8, other arithmetic, add_group(): total + cross_block(left_rows, turned_rows, right_rows).astype(jnp.float32)  53.2 us
    dot_general x8, matrix products, cross_block(): jnp.einsum('sik,sjk->ijk', local_spec, remote_spec, preferred_element_typ...  16.6 us
    dot_general x1, matrix products, per_device(): jnp.einsum('ijk,kl->ijl', summed, table.astype(jnp.float32), precision=la...  14.2 us
  transfers between devices with their start and end apart: 8, of which 7 were waited for; matrix products, arithmetic and copies ran while one was open for 1% of the time, Pallas kernels for 0%

profile of v1, /device:TPU:0, one launch (start us, length us, event | category | flops | bytes accessed | tf_op | source)
XLA Modules:
  0.0 590.9 jit_solution(5452748174097003109)
XLA Ops:
  6.5 70.9 %slice.23 = f32[4,128,1024]{2,1,0:T(8,128)S(1)} slice(f32[4,128,2048]{2,1,0:T(8,128)} %param.3), slice={[0:4:1], [0:128:1], [1:2048:2]} | slice | bytes 4194304 | tf_op jit(solution)/shard_map/slice | solution.py:17
  77.4 71.3 %slice.25 = f32[4,128,1024]{2,1,0:T(8,128)} slice(f32[4,128,2048]{2,1,0:T(8,128)} %param.3), slice={[0:4:1], [0:128:1], [0:2048:2]} | slice | bytes 4194304 | tf_op jit(solution)/shard_map/slice | solution.py:16
  148.7 5.7 fusion.14
  154.5 4.1 fusion.24
  159.5 4.1 collective-permute-start.1
  163.6 4.2 collective-permute-done
  168.3 3.8 collective-permute-start.3
  177.2 3.7 collective-permute-start.5
  184.9 2.6 collective-permute-done.5
  188.3 3.6 collective-permute-done.6
  192.7 3.7 dynamic-slice_select_fusion
  197.0 69.2 %all-reduce.3.cloned.1.call-done = bf16[2,32,64,128]{2,1,3,0:T(8,128)(2,1)} async-done(((bf16[2,32,64,128]{2,1,3,0:T(8,128)(2,1)}), bf16[2,32,64,128]{2,1,3,0:T(8,128)(2,1)}) %all-reduce.3.cloned.1.call-update) | async-done | bytes 1048592 | tf_op jit(solution)/shard_map/psum | solution.py:12
  266.2 106.2 %while.14 = (s32[]{:T(128)}, f32[128,64,256]{0,1,2:T(8,128)}, bf16[2,32,64,128]{2,1,3,0:T(8,128)(2,1)}, bf16[2,32,128,128]{2,1,3,0:T(8,128)(2,1)}, s32[]{:T(128)}, /*index=5*/s32[]{:T(128)}, s32[]{:T(128)}, s32[]{:T(128)}, s32[]{}) while((s32[]{:T(128)}, f32[128,64,256]{0,1,2:T(8,128)}, bf16[2,32,64,128]{2,1,3,0:T(8,128)(2,1)}, ...), condition=%wide.region_3.4_spmd.clone, body=%wide.region_2.3_spmd.clone.sunk | while | flops 44761096 | bytes 28049584 | solution.py:109
  270.8 2.1 convert_bitcast_fusion.5
  272.9 5.3 select_add_fusion.2
  282.7 2.1 convert_bitcast_fusion.5
  284.8 6.8 %select_add_fusion.2 = f32[128,64,256]{0,1,2:T(8,128)} fusion(f32[128,64,256]{0,1,2:T(8,128)} %get-tuple-element.163, bf16[128,64,128]{0,1,2:T(8,128)(2,1)S(1)} %convert_bitcast_fusion.4, bf16[128,64,128]{0,1,2:T(8,128)(2,1)} %convert_bitcast_fusion.5, pred[]{:T(512)S(6)} %compare.20), kind=kLoop, calls=%fused_computation.clone.1 | loop fusion | flops 8388608 | bytes 20971520 | tf_op jit(solution)/shard_map/while/body/eval_jaxpr/add | solution.py:107
  296.2 2.1 convert_bitcast_fusion.5
  298.2 6.8 %select_add_fusion.2 = f32[128,64,256]{0,1,2:T(8,128)} fusion(f32[128,64,256]{0,1,2:T(8,128)} %get-tuple-element.163, bf16[128,64,128]{0,1,2:T(8,128)(2,1)S(1)} %convert_bitcast_fusion.4, bf16[128,64,128]{0,1,2:T(8,128)(2,1)} %convert_bitcast_fusion.5, pred[]{:T(512)S(6)} %compare.20), kind=kLoop, calls=%fused_computation.clone.1 | loop fusion | flops 8388608 | bytes 20971520 | tf_op jit(solution)/shard_map/while/body/eval_jaxpr/add | solution.py:107
  309.6 2.1 convert_bitcast_fusion.5
  311.7 6.8 %select_add_fusion.2 = f32[128,64,256]{0,1,2:T(8,128)} fusion(f32[128,64,256]{0,1,2:T(8,128)} %get-tuple-element.163, bf16[128,64,128]{0,1,2:T(8,128)(2,1)S(1)} %convert_bitcast_fusion.4, bf16[128,64,128]{0,1,2:T(8,128)(2,1)} %convert_bitcast_fusion.5, pred[]{:T(512)S(6)} %compare.20), kind=kLoop, calls=%fused_computation.clone.1 | loop fusion | flops 8388608 | bytes 20971520 | tf_op jit(solution)/shard_map/while/body/eval_jaxpr/add | solution.py:107
  323.1 2.1 convert_bitcast_fusion.5
  325.2 6.8 %select_add_fusion.2 = f32[128,64,256]{0,1,2:T(8,128)} fusion(f32[128,64,256]{0,1,2:T(8,128)} %get-tuple-element.163, bf16[128,64,128]{0,1,2:T(8,128)(2,1)S(1)} %convert_bitcast_fusion.4, bf16[128,64,128]{0,1,2:T(8,128)(2,1)} %convert_bitcast_fusion.5, pred[]{:T(512)S(6)} %compare.20), kind=kLoop, calls=%fused_computation.clone.1 | loop fusion | flops 8388608 | bytes 20971520 | tf_op jit(solution)/shard_map/while/body/eval_jaxpr/add | solution.py:107
  336.5 2.1 convert_bitcast_fusion.5
  338.6 6.8 %select_add_fusion.2 = f32[128,64,256]{0,1,2:T(8,128)} fusion(f32[128,64,256]{0,1,2:T(8,128)} %get-tuple-element.163, bf16[128,64,128]{0,1,2:T(8,128)(2,1)S(1)} %convert_bitcast_fusion.4, bf16[128,64,128]{0,1,2:T(8,128)(2,1)} %convert_bitcast_fusion.5, pred[]{:T(512)S(6)} %compare.20), kind=kLoop, calls=%fused_computation.clone.1 | loop fusion | flops 8388608 | bytes 20971520 | tf_op jit(solution)/shard_map/while/body/eval_jaxpr/add | solution.py:107
  350.0 2.1 convert_bitcast_fusion.5
  352.1 6.8 %select_add_fusion.2 = f32[128,64,256]{0,1,2:T(8,128)} fusion(f32[128,64,256]{0,1,2:T(8,128)} %get-tuple-element.163, bf16[128,64,128]{0,1,2:T(8,128)(2,1)S(1)} %convert_bitcast_fusion.4, bf16[128,64,128]{0,1,2:T(8,128)(2,1)} %convert_bitcast_fusion.5, pred[]{:T(512)S(6)} %compare.20), kind=kLoop, calls=%fused_computation.clone.1 | loop fusion | flops 8388608 | bytes 20971520 | tf_op jit(solution)/shard_map/while/body/eval_jaxpr/add | solution.py:107
  365.6 6.8 %select_add_fusion.2 = f32[128,64,256]{0,1,2:T(8,128)} fusion(f32[128,64,256]{0,1,2:T(8,128)} %get-tuple-element.163, bf16[128,64,128]{0,1,2:T(8,128)(2,1)S(1)} %convert_bitcast_fusion.4, bf16[128,64,128]{0,1,2:T(8,128)(2,1)} %convert_bitcast_fusion.5, pred[]{:T(512)S(6)} %compare.20), kind=kLoop, calls=%fused_computation.clone.1 | loop fusion | flops 8388608 | bytes 20971520 | tf_op jit(solution)/shard_map/while/body/eval_jaxpr/add | solution.py:107
  372.4 14.2 %broadcast_multiply_fusion = f32[128,64,256]{2,0,1:T(8,128)S(1)} fusion(f32[128,64,256]{0,1,2:T(8,128)} %get-tuple-element.84, bf16[128,256]{1,0:T(8,128)(2,1)S(1)} %get-tuple-element.121, bf16[128,256]{1,0:T(8,128)(2,1)S(1)} %get-tuple-element.120), kind=kOutput, calls=%fused_computation.14 | convolution fusion | flops 6444810240 | bytes 16908288 | tf_op jit(solution)/shard_map/ijk,kl->ijl/dot_general | solution.py:113
  386.6 4.9 copy.15
  391.5 188.5 %all_to_all.18 = f32[128,64,256]{2,1,0:T(8,128)S(1)} all-to-all(f32[128,64,256]{2,1,0:T(8,128)S(1)} %copy.15), channel_id=1, replica_groups=mesh['chan'=4,'tm'=8] {'tm'}, dimensions={0} | all-to-all | bytes 16777216 | tf_op jit(solution)/shard_map/all_to_all | solution.py:118
  580.0 4.0 copy.16
  (78 shorter events, 50.9 us)
Async XLA Ops:
  6.5 259.7 %all-reduce.3.cloned.1.call-start = ((), (), s32[]{:S(2)}) async-start(), calls=%async_computation.1 | async-start | bytes 4194304 | tf_op jit(solution)/shard_map/psum | solution.py:12
  148.7 5.8 copy-start
  159.0 8.8 %collective-permute-start = (bf16[2,4,128,128]{2,1,3,0:T(4,128)(2,1)S(1)}, bf16[2,4,128,128]{2,1,3,0:T(4,128)(2,1)S(1)}, u32[]{:S(2)}, u32[]{:S(2)}) collective-permute-start(bf16[2,4,128,128]{2,1,3,0:T(4,128)(2,1)S(1)} %copy.10), channel_id=1, source_target_pairs={{0,1},{1,2},{2,3},{3,4},{4,5},{5,6},{6,7},{7,0},{8,9},{9,10},{10,1... | collective-permute-start | bytes 786440 | tf_op jit(solution)/shard_map/ppermute | solution.py:85
  159.5 8.7 %collective-permute-start.1 = (bf16[2,4,128,128]{2,1,3,0:T(4,128)(2,1)S(1)}, bf16[2,4,128,128]{2,1,3,0:T(4,128)(2,1)S(1)}, u32[]{:S(2)}, u32[]{:S(2)}) collective-permute-start(bf16[2,4,128,128]{2,1,3,0:T(4,128)(2,1)S(1)} %copy.10), channel_id=1, source_target_pairs={{0,7},{1,0},{2,1},{3,2},{4,3},{5,4},{6,5},{7,6},{8,15},{9,8},{10,9... | collective-permute-start | bytes 786440 | tf_op jit(solution)/shard_map/ppermute | solution.py:90
  167.8 7.7 %collective-permute-start.2 = (bf16[2,4,128,128]{2,1,3,0:T(4,128)(2,1)S(1)}, bf16[2,4,128,128]{2,1,3,0:T(4,128)(2,1)S(1)}, u32[]{:S(2)}, u32[]{:S(2)}) collective-permute-start(bf16[2,4,128,128]{2,1,3,0:T(4,128)(2,1)S(1)} %collective-permute-done), channel_id=1, source_target_pairs={{0,1},{1,2},{2,3},{3,4},{4,5},{5,6},{6,7},{7,0},{8,9},{9,10},{10,1... | collective-permute-start | bytes 786440 | tf_op jit(solution)/shard_map/ppermute | solution.py:85
  168.3 8.9 %collective-permute-start.3 = (bf16[2,4,128,128]{2,1,3,0:T(4,128)(2,1)S(1)}, bf16[2,4,128,128]{2,1,3,0:T(4,128)(2,1)S(1)}, u32[]{:S(2)}, u32[]{:S(2)}) collective-permute-start(bf16[2,4,128,128]{2,1,3,0:T(4,128)(2,1)S(1)} %collective-permute-done.1), channel_id=1, source_target_pairs={{0,7},{1,0},{2,1},{3,2},{4,3},{5,4},{6,5},{7,6},{8,15},{9,8},{10,9... | collective-permute-start | bytes 786440 | tf_op jit(solution)/shard_map/ppermute | solution.py:90
  175.5 7.7 %collective-permute-start.4 = (bf16[2,4,128,128]{2,1,3,0:T(4,128)(2,1)S(1)}, bf16[2,4,128,128]{2,1,3,0:T(4,128)(2,1)S(1)}, u32[]{:S(2)}, u32[]{:S(2)}) collective-permute-start(bf16[2,4,128,128]{2,1,3,0:T(4,128)(2,1)S(1)} %collective-permute-done.2), channel_id=1, source_target_pairs={{0,1},{1,2},{2,3},{3,4},{4,5},{5,6},{6,7},{7,0},{8,9},{9,10},{10,1... | collective-permute-start | bytes 786440 | tf_op jit(solution)/shard_map/ppermute | solution.py:85
  177.2 10.3 %collective-permute-start.5 = (bf16[2,4,128,128]{2,1,3,0:T(4,128)(2,1)S(1)}, bf16[2,4,128,128]{2,1,3,0:T(4,128)(2,1)S(1)}, u32[]{:S(2)}, u32[]{:S(2)}) collective-permute-start(bf16[2,4,128,128]{2,1,3,0:T(4,128)(2,1)S(1)} %collective-permute-done.3), channel_id=1, source_target_pairs={{0,7},{1,0},{2,1},{3,2},{4,3},{5,4},{6,5},{7,6},{8,15},{9,8},{10,9... | collective-permute-start | bytes 786440 | tf_op jit(solution)/shard_map/ppermute | solution.py:90
  183.2 8.6 %collective-permute-start.6 = (bf16[2,4,128,128]{2,1,3,0:T(4,128)(2,1)S(1)}, bf16[2,4,128,128]{2,1,3,0:T(4,128)(2,1)S(1)}, u32[]{:S(2)}, u32[]{:S(2)}) collective-permute-start(bf16[2,4,128,128]{2,1,3,0:T(4,128)(2,1)S(1)} %collective-permute-done.4), channel_id=1, source_target_pairs={{0,1},{1,2},{2,3},{3,4},{4,5},{5,6},{6,7},{7,0},{8,9},{9,10},{10,1... | collective-permute-start | bytes 786440 | tf_op jit(solution)/shard_map/ppermute | solution.py:85
Sparse Core Ops, SparseCore 0:
  196.5 69.6 all-reduce.2
